TPU v7x, 32 devices: a whole 2x2x4 slice. The times are simulated.
32 devices in a mesh: space: 8 (over z, y), chan: 4 (over x, core).
Axes of the slice: x: 2, y: 2, z: 4, core: 2. Of those that a mesh axis runs over, the one named last changes fastest.
Arguments:
- positions: float32 [3, 2048], P(None, 'space'), may hold values from 0 to 2
- features: bfloat16 [128, 2048], P('chan', 'space'), may hold values from -6 to 6
- send_rows: int32 [24, 128], P('space'), may hold values from 0 to 255, as said below
- pair_tiles: int32 [64, 2], P('space'), may hold values from 0 to 4, as said below
- tile_live: int32 [64], P('space'), may hold values from 0 to 1, as said below
- radial_weight: float32 [128, 8], P('chan'), may hold values from -1 to 1
- mix_weight: bfloat16 [3, 128, 128], replicated, may hold values from -0.5 to 0.5
- out_grad: bfloat16 [128, 9, 2048], P('chan', None, 'space'), may hold values from -6 to 6
Outputs:
- output: bfloat16 [128, 9, 2048], P('chan', None, 'space')
- grad_features: bfloat16 [128, 2048], P('chan', 'space')
- forces: float32 [3, 2048], P(None, 'space')
- grad_radial: float32 [128, 8], P('chan')
Inputs may be any that keep to these rules, and one draw needn't show every extreme that they name: `send_rows`: row s * 3 + b lists 128 distinct atoms of domain s, numbered within the domain, that domain s sends to domain s xor 2^b. `pair_tiles`: row s * 8 + t holds domain s's tile t: a target block below 2 among its own blocks, then a source block below 5 among its source blocks. `tile_live`: on each domain the live tiles come first; each domain has 2 or more live tiles, and some domain has all 8.
All inputs are finite; a program needn't handle non-finite values.
Results may differ from a plain program's by a relative error of at most 0.025.
Values may be sent and summed in bfloat16 or wider, within the bound.
No kernel may reach another device: no remote copies, remote signals or barrier semaphores. Data moves between devices by JAX's collectives and lax.ppermute only.
A program may use at most 64 MiB of HBM per device.

v0:
```python
import math
import jax
import jax.numpy as jnp
from jax import lax
from jax.sharding import PartitionSpec as P

SOFTENING = 0.25
CUTOFF = 2.5
CUTOFF_SQ = 6.25
SHARPNESS = 10.0
ROOT_THREE = math.sqrt(3.0)
ORDER_OF = (0, 1, 1, 1, 2, 2, 2, 2, 2)


def partner(value, axis, bit):
    mask = 2**bit
    pairs = [(source, source ^ mask) for source in range(lax.axis_size(axis))]
    return lax.ppermute(value, axis, pairs)


def geometry(target_pos, source_pos, pair_keep, radial_count):
    offset = source_pos[:, None, :] - target_pos[:, :, None]
    dist_sq = jnp.sum(offset * offset, axis=0) + SOFTENING
    distance = jnp.sqrt(dist_sq)
    along_x = offset[0] / distance
    along_y = offset[1] / distance
    along_z = offset[2] / distance
    harmonics = jnp.stack(
        [
            jnp.ones_like(along_x),
            along_x,
            along_y,
            along_z,
            ROOT_THREE * along_x * along_y,
            ROOT_THREE * along_y * along_z,
            ROOT_THREE * along_x * along_z,
            0.5 * (3.0 * along_z * along_z - 1.0),
            0.5 * ROOT_THREE * (along_x * along_x - along_y * along_y),
        ]
    )
    envelope = jnp.square(jnp.maximum(1.0 - dist_sq / CUTOFF_SQ, 0.0)) * pair_keep
    centers = (jnp.arange(radial_count, dtype=jnp.float32) + 0.5) * (CUTOFF / radial_count)
    radial = (
        jnp.exp(-SHARPNESS * jnp.square(distance[None] - centers[:, None, None])) * envelope[None]
    )
    return (harmonics, radial)


def take_block(array, blk_index, block_size):
    return lax.dynamic_slice_in_dim(array, blk_index * block_size, block_size, array.ndim - 1)


def add_block(array, blk_index, value, block_size):
    current = take_block(array, blk_index, block_size)
    return lax.dynamic_update_slice_in_dim(
        array, current + value, blk_index * block_size, array.ndim - 1
    )


def body(
    positions, features, send_rows, pair_tiles, tile_live, radial_weight, mix_weight, out_grad
):
    block_size = send_rows.shape[1]
    atoms_dev = positions.shape[1]
    chan_dev = features.shape[0]
    radial_count = radial_weight.shape[1]
    components = out_grad.shape[1]
    levels = lax.axis_size("space").bit_length() - 1
    pos_list = [positions]
    feat_list = [features]
    for level_bit in range(levels):
        sent_rows = send_rows[level_bit]
        got_feat, got_pos = (
            partner(
                jnp.take(features, sent_rows, axis=1).astype(jnp.float32), "space", level_bit
            ).astype(jnp.bfloat16),
            partner(jnp.take(positions, sent_rows, axis=1), "space", level_bit),
        )
        feat_list.append(got_feat)
        pos_list.append(got_pos)
    src_pos = jnp.concatenate(pos_list, axis=1)
    src_feat = jnp.concatenate(feat_list, axis=1)
    src_atoms = src_pos.shape[1]
    live_count = jnp.sum(tile_live)

    def tile_parts(tile_index):
        target_blk = pair_tiles[tile_index, 0]
        source_blk = pair_tiles[tile_index, 1]
        same = (target_blk == source_blk).astype(jnp.float32)
        pair_keep = 1.0 - same * jnp.eye(block_size, dtype=jnp.float32)
        target_pos = take_block(src_pos, target_blk, block_size)
        source_pos = take_block(src_pos, source_blk, block_size)

        def geo_fn(first_pos, second_pos):
            return geometry(first_pos, second_pos, pair_keep, radial_count)

        return (target_blk, source_blk, target_pos, source_pos, geo_fn)

    def forward_tile(tile_index, moments):
        target_blk, source_blk, target_pos, source_pos, geo_fn = tile_parts(tile_index)
        harmonics, radial = geo_fn(target_pos, source_pos)
        source_feat = take_block(src_feat, source_blk, block_size)
        pieces_list = []
        for harmonic in range(components):
            pair_values = (harmonics[harmonic][None] * radial).astype(jnp.bfloat16)
            message = jnp.einsum(
                "kij,cj->cki", pair_values, source_feat, preferred_element_type=jnp.float32
            )
            pieces_list.append(jnp.einsum("cki,ck->ci", message, radial_weight))
        contrib = jnp.stack(pieces_list, axis=1)
        return add_block(moments, target_blk, contrib, block_size)

    moments = lax.fori_loop(
        0, live_count, forward_tile, jnp.zeros((chan_dev, components, atoms_dev), jnp.float32)
    )
    packed = moments.astype(jnp.bfloat16)
    mixing = jnp.take(mix_weight, jnp.array(ORDER_OF, dtype=jnp.int32), axis=0)
    offset = lax.axis_index("chan") * chan_dev
    gathered_piece = lax.all_gather(packed, "chan", axis=0, tiled=True)
    weight_part = lax.dynamic_slice(
        mixing, (0, offset, 0), (components, chan_dev, gathered_piece.shape[0])
    )
    mixed_out = jnp.einsum(
        "lxc,cli->xli", weight_part, gathered_piece, preferred_element_type=jnp.float32
    )
    scalar_part = mixed_out[:, 0, :]
    gate_value = jax.nn.sigmoid(scalar_part)
    result = jnp.concatenate(
        [(scalar_part * gate_value)[:, None, :], mixed_out[:, 1:, :] * gate_value[:, None, :]],
        axis=1,
    ).astype(jnp.bfloat16)
    upstream = out_grad.astype(jnp.float32)
    scalar_grad = upstream[:, 0, :] * (
        gate_value * (1.0 + scalar_part * (1.0 - gate_value))
    ) + gate_value * (1.0 - gate_value) * jnp.sum(upstream[:, 1:, :] * mixed_out[:, 1:, :], axis=1)
    rest_grad = upstream[:, 1:, :] * gate_value[:, None, :]
    dz_packed = jnp.concatenate([scalar_grad[:, None, :], rest_grad], axis=1).astype(jnp.bfloat16)
    gathered_piece = lax.all_gather(dz_packed, "chan", axis=0, tiled=True)
    weight_part = lax.dynamic_slice(
        mixing, (0, 0, offset), (components, gathered_piece.shape[0], chan_dev)
    )
    moment_grad_all = jnp.einsum(
        "lxc,xli->cli", weight_part, gathered_piece, preferred_element_type=jnp.float32
    )

    def backward_tile(tile_index, running):
        grad_src, dpos_src, grad_rad = running
        target_blk, source_blk, target_pos, source_pos, geo_fn = tile_parts(tile_index)
        (harmonics, radial), pullback = jax.vjp(geo_fn, target_pos, source_pos)
        source_feat = take_block(src_feat, source_blk, block_size)
        moment_grad = take_block(moment_grad_all, target_blk, block_size)
        grad_source = jnp.zeros((chan_dev, block_size), jnp.float32)
        rad_grad = jnp.zeros_like(radial)
        harm_list = []
        for harmonic in range(components):
            pair_values = (harmonics[harmonic][None] * radial).astype(jnp.bfloat16)
            message = jnp.einsum(
                "kij,cj->cki", pair_values, source_feat, preferred_element_type=jnp.float32
            )
            grad_rad = grad_rad + jnp.einsum("cki,ci->ck", message, moment_grad[:, harmonic, :])
            weighted = (radial_weight[:, :, None] * moment_grad[:, harmonic, None, :]).astype(
                jnp.bfloat16
            )
            grad_source = grad_source + jnp.einsum(
                "cki,kij->cj", weighted, pair_values, preferred_element_type=jnp.float32
            )
            value_grad = jnp.einsum(
                "cki,cj->kij", weighted, source_feat, preferred_element_type=jnp.float32
            )
            harm_list.append(jnp.sum(value_grad * radial, axis=0))
            rad_grad = rad_grad + value_grad * harmonics[harmonic][None]
        target_grad, source_grad_pos = pullback((jnp.stack(harm_list), rad_grad))
        grad_src = add_block(grad_src, source_blk, grad_source, block_size)
        dpos_src = add_block(dpos_src, target_blk, target_grad, block_size)
        dpos_src = add_block(dpos_src, source_blk, source_grad_pos, block_size)
        return (grad_src, dpos_src, grad_rad)

    init = (
        jnp.zeros((chan_dev, src_atoms), jnp.float32),
        jnp.zeros((3, src_atoms), jnp.float32),
        jnp.zeros((chan_dev, radial_count), jnp.float32),
    )
    grad_src, dpos_src, grad_rad = lax.fori_loop(0, live_count, backward_tile, init)
    dpos_src = lax.psum(dpos_src, "chan")
    own_grad = grad_src[:, :atoms_dev]
    own_dpos = dpos_src[:, :atoms_dev]
    for level_bit in range(levels):
        low = atoms_dev + level_bit * block_size
        back_grad, back_pos = partner(
            (grad_src[:, low : low + block_size], dpos_src[:, low : low + block_size]),
            "space",
            level_bit,
        )
        sent_rows = send_rows[level_bit]
        own_grad = own_grad.at[:, sent_rows].add(back_grad)
        own_dpos = own_dpos.at[:, sent_rows].add(back_pos)
    grad_radial = lax.psum(grad_rad, "space")
    return (result, own_grad.astype(jnp.bfloat16), -own_dpos, grad_radial)


def solution(mesh):
    placed = (
        P(None, "space"),
        P("chan", "space"),
        P("space", None),
        P("space", None),
        P("space"),
        P("chan", None),
        P(),
        P("chan", None, "space"),
    )
    return jax.shard_map(
        body,
        mesh=mesh,
        in_specs=placed,
        out_specs=(P("chan", None, "space"), P("chan", "space"), P(None, "space"), P("chan", None)),
        check_vma=False,
    )
```

profile of v0, /device:TPU:0, one launch (start us, length us, event | category | flops | bytes accessed | tf_op | source)
XLA Modules:
  0.0 354.6 jit_solution(2762358216147547025)
XLA Ops:
  2.4 4.1 %collective-permute-start.2 = (bf16[32,128]{1,0:T(8,128)(2,1)S(1)}, bf16[32,128]{1,0:T(8,128)(2,1)S(1)}, u32[]{:S(2)}, u32[]{:S(2)}) collective-permute-start(bf16[32,128]{1,0:T(8,128)(2,1)S(1)} %bitcast_convert_fusion), channel_id=1, source_target_pairs={{0,16},{4,20},{8,24},{12,28},{16,0},{20,4},{24,8},{28,12},{1,17},{... | collective-permute-start | bytes 24584 | tf_op jit(solution)/shard_map/ppermute | solution.py:18
  7.3 1.6 collective-permute-start.1
  12.4 1.6 collective-permute-start.3
  18.2 2.9 collective-permute-done
  21.8 19.3 %while.28 = (s32[]{:T(128)}, f32[32,9,256]{2,0,1:T(8,128)S(1)}, s32[]{:T(128)}, s32[8,2]{0,1:T(2,128)S(1)}, bf16[32,640]{1,0:T(8,128)(2,1)S(1)}, /*index=5*/f32[...) while((s32[]{:T(128)}, f32[32,9,256]{2,0,1:T(8,128)S(1)}, ...), condition=%wide.region_3.6_spmd, body=%wide.region_1.5_spmd.sunk | while | flops 83677216 | bytes 5811606 | solution.py:113
  41.7 7.5 %all_gather.6 = bf16[128,9,256]{2,0,1:T(8,128)(2,1)S(1)} all-gather(bf16[32,9,256]{2,0,1:T(8,128)(2,1)S(1)} %convert_element_type.217), channel_id=1, replica_groups=mesh['space'=8,'chan'=4] {'chan'}, dimensions={0}, use_global_device_ids=true | all-gather | bytes 737280 | tf_op jit(solution)/shard_map/all_gather | solution.py:119
  49.6 7.6 %all_gather.7 = bf16[128,9,256]{2,0,1:T(8,128)(2,1)S(1)} all-gather(bf16[32,9,256]{2,0,1:T(8,128)(2,1)S(1)} %pad_maximum_fusion.1), channel_id=1, replica_groups=mesh['space'=8,'chan'=4] {'chan'}, dimensions={0}, use_global_device_ids=true | all-gather | bytes 737280 | tf_op jit(solution)/shard_map/all_gather | solution.py:138
  57.7 47.2 %while.29 = (s32[]{:T(128)}, f32[32,640]{1,0:T(8,128)S(1)}, f32[3,640]{1,0:T(4,128)S(1)}, f32[32,8]{0,1:T(8,128)S(1)}, s32[]{:T(128)}, /*index=5*/s32[8,2]{0,1:T...) while((s32[]{:T(128)}, f32[32,640]{1,0:T(8,128)S(1)}, ...), condition=%wide.region_19.22_spmd, body=%wide.region_5.21_spmd.sunk | while | flops 250567328 | bytes 19222200 | solution.py:183
  68.5 1.3 fusion.574
  75.4 1.0 fusion.586
  76.7 1.0 fusion.588
  91.7 1.3 fusion.574
  105.1 14.2 %psum.14 = f32[3,640]{0,1:T(8,128)S(1)} all-reduce(f32[3,640]{0,1:T(8,128)S(1)} %copy.73), channel_id=1, replica_groups=mesh['space'=8,'chan'=4] {'chan'}, use_global_device_ids=true, to_apply=%region_23.26 | all-reduce | flops 1920 | bytes 15360 | tf_op jit(solution)/shard_map/psum | solution.py:184
  119.3 195.9 %collective-permute-start.9 = (f32[3,128]{0,1:T(8,128)S(1)}, f32[3,128]{0,1:T(8,128)S(1)}, u32[]{:S(2)}, u32[]{:S(2)}) collective-permute-start(f32[3,128]{0,1:T(8,128)S(1)} %get-tuple-element.342), channel_id=1, source_target_pairs={{0,4},{4,0},{8,12},{12,8},{16,20},{20,16},{24,28},{28,24},{1,5},{5... | collective-permute-start | bytes 4616 | tf_op jit(solution)/shard_map/ppermute | solution.py:18
  315.3 2.9 collective-permute-start.7
  318.2 1.1 collective-permute-start.8
  319.3 2.0 collective-permute-start.10
  323.1 21.2 %psum.15 = f32[32,8]{0,1:T(8,128)} all-reduce(f32[32,8]{0,1:T(8,128)S(1)} %get-tuple-element.231), channel_id=1, replica_groups=mesh['space'=8,'chan'=4] {'space'}, use_global_device_ids=true, to_apply=%region_27.30 | all-reduce | flops 256 | bytes 2048 | tf_op jit(solution)/shard_map/psum | solution.py:197
  344.3 1.3 scatter_custom_fusion.3
  345.6 1.3 scatter_custom_fusion.4
  347.0 1.3 scatter_custom_fusion.5
  349.9 1.3 scatter_fusion
  351.2 1.3 scatter_fusion.1
  352.5 1.3 scatter_fusion.2
  (273 shorter events, 62.9 us)
Async XLA Ops:
  0.6 16.1 %copy-start = (bf16[3,128,128]{2,1,0:T(8,128)(2,1)S(1)}, bf16[3,128,128]{2,1,0:T(8,128)(2,1)}, u32[]{:S(2)}) copy-start(bf16[3,128,128]{2,1,0:T(8,128)(2,1)} %param.23) | copy-start | bytes 294916
  0.6 0.9 copy-start.10
  2.4 15.8 %collective-permute-start.2 = (bf16[32,128]{1,0:T(8,128)(2,1)S(1)}, bf16[32,128]{1,0:T(8,128)(2,1)S(1)}, u32[]{:S(2)}, u32[]{:S(2)}) collective-permute-start(bf16[32,128]{1,0:T(8,128)(2,1)S(1)} %bitcast_convert_fusion), channel_id=1, source_target_pairs={{0,16},{4,20},{8,24},{12,28},{16,0},{20,4},{24,8},{28,12},{1,17},{... | collective-permute-start | bytes 24584 | tf_op jit(solution)/shard_map/ppermute | solution.py:18
  7.3 1.7 copy-start.9
  7.3 10.9 %collective-permute-start.1 = (bf16[32,128]{1,0:T(8,128)(2,1)S(1)}, bf16[32,128]{1,0:T(8,128)(2,1)S(1)}, u32[]{:S(2)}, u32[]{:S(2)}) collective-permute-start(bf16[32,128]{1,0:T(8,128)(2,1)S(1)} %bitcast_convert_fusion.1), channel_id=1, source_target_pairs={{0,8},{4,12},{8,0},{12,4},{16,24},{20,28},{24,16},{28,20},{1,9},{5... | collective-permute-start | bytes 24584 | tf_op jit(solution)/shard_map/ppermute | solution.py:18
  9.8 7.5 %collective-permute-start.5 = (f32[3,128]{0,1:T(8,128)S(1)}, f32[3,128]{0,1:T(8,128)S(1)}, u32[]{:S(2)}, u32[]{:S(2)}) collective-permute-start(f32[3,128]{0,1:T(8,128)S(1)} %select_bitcast_fusion), channel_id=1, source_target_pairs={{0,16},{4,20},{8,24},{12,28},{16,0},{20,4},{24,8},{28,12},{1,17},{... | collective-permute-start | bytes 4616 | tf_op jit(solution)/shard_map/ppermute | solution.py:18
  11.0 7.0 %collective-permute-start.4 = (f32[3,128]{0,1:T(8,128)S(1)}, f32[3,128]{0,1:T(8,128)S(1)}, u32[]{:S(2)}, u32[]{:S(2)}) collective-permute-start(f32[3,128]{0,1:T(8,128)S(1)} %select_bitcast_fusion.1), channel_id=1, source_target_pairs={{0,8},{4,12},{8,0},{12,4},{16,24},{20,28},{24,16},{28,20},{1,9},{5... | collective-permute-start | bytes 4616 | tf_op jit(solution)/shard_map/ppermute | solution.py:18
  11.6 3.8 %copy-start.6 = (bf16[32,9,256]{2,0,1:T(8,128)(2,1)S(1)}, bf16[32,9,256]{2,0,1:T(8,128)(2,1)}, u32[]{:S(2)}) copy-start(bf16[32,9,256]{2,0,1:T(8,128)(2,1)} %param.24) | copy-start | bytes 442372
  12.4 5.7 %collective-permute-start.3 = (f32[3,128]{0,1:T(8,128)S(1)}, f32[3,128]{0,1:T(8,128)S(1)}, u32[]{:S(2)}, u32[]{:S(2)}) collective-permute-start(f32[3,128]{0,1:T(8,128)S(1)} %select_bitcast_fusion.2), channel_id=1, source_target_pairs={{0,4},{4,0},{8,12},{12,8},{16,20},{20,16},{24,28},{28,24},{1,5},{5... | collective-permute-start | bytes 4616 | tf_op jit(solution)/shard_map/ppermute | solution.py:18
  15.4 1.3 copy-start.1
  17.4 3.7 %collective-permute-start = (bf16[32,128]{1,0:T(8,128)(2,1)S(1)}, bf16[32,128]{1,0:T(8,128)(2,1)S(1)}, u32[]{:S(2)}, u32[]{:S(2)}) collective-permute-start(bf16[32,128]{1,0:T(8,128)(2,1)S(1)} %bitcast_convert_fusion.2), channel_id=1, source_target_pairs={{0,4},{4,0},{8,12},{12,8},{16,20},{20,16},{24,28},{28,24},{1,5},{5... | collective-permute-start | bytes 24584 | tf_op jit(solution)/shard_map/ppermute | solution.py:18
  18.2 2.9 copy-start.8
  64.9 0.8 copy-start.3
  88.1 0.8 copy-start.3
  119.3 203.1 %copy-start.5 = (f32[3,640]{0,1:T(8,128)}, f32[3,640]{0,1:T(8,128)S(1)}, u32[]{:S(2)}) copy-start(f32[3,640]{0,1:T(8,128)S(1)} %psum.14) | copy-start | bytes 23044
  119.3 202.0 %collective-permute-start.9 = (f32[3,128]{0,1:T(8,128)S(1)}, f32[3,128]{0,1:T(8,128)S(1)}, u32[]{:S(2)}, u32[]{:S(2)}) collective-permute-start(f32[3,128]{0,1:T(8,128)S(1)} %get-tuple-element.342), channel_id=1, source_target_pairs={{0,4},{4,0},{8,12},{12,8},{16,20},{20,16},{24,28},{28,24},{1,5},{5... | collective-permute-start | bytes 4616 | tf_op jit(solution)/shard_map/ppermute | solution.py:18
  315.2 33.8 %collective-permute-start.6 = (f32[32,128]{1,0:T(8,128)S(1)}, f32[32,128]{1,0:T(8,128)S(1)}, u32[]{:S(2)}, u32[]{:S(2)}) collective-permute-start(f32[32,128]{1,0:T(8,128)S(1)} %get-tuple-element.348), channel_id=1, source_target_pairs={{0,4},{4,0},{8,12},{12,8},{16,20},{20,16},{24,28},{28,24},{1,5},{5... | collective-permute-start | bytes 49160 | tf_op jit(solution)/shard_map/ppermute | solution.py:18
  315.3 33.8 %collective-permute-start.7 = (f32[32,128]{1,0:T(8,128)S(1)}, f32[32,128]{1,0:T(8,128)S(1)}, u32[]{:S(2)}, u32[]{:S(2)}) collective-permute-start(f32[32,128]{1,0:T(8,128)S(1)} %get-tuple-element.347), channel_id=1, source_target_pairs={{0,8},{4,12},{8,0},{12,4},{16,24},{20,28},{24,16},{28,20},{1,9},{5... | collective-permute-start | bytes 49160 | tf_op jit(solution)/shard_map/ppermute | solution.py:18
  318.2 31.0 %collective-permute-start.8 = (f32[32,128]{1,0:T(8,128)S(1)}, f32[32,128]{1,0:T(8,128)S(1)}, u32[]{:S(2)}, u32[]{:S(2)}) collective-permute-start(f32[32,128]{1,0:T(8,128)S(1)} %get-tuple-element.346), channel_id=1, source_target_pairs={{0,16},{4,20},{8,24},{12,28},{16,0},{20,4},{24,8},{28,12},{1,17},{... | collective-permute-start | bytes 49160 | tf_op jit(solution)/shard_map/ppermute | solution.py:18
  319.3 26.3 %collective-permute-start.10 = (f32[3,128]{0,1:T(8,128)S(1)}, f32[3,128]{0,1:T(8,128)S(1)}, u32[]{:S(2)}, u32[]{:S(2)}) collective-permute-start(f32[3,128]{0,1:T(8,128)S(1)} %get-tuple-element.341), channel_id=1, source_target_pairs={{0,8},{4,12},{8,0},{12,4},{16,24},{20,28},{24,16},{28,20},{1,9},{5... | collective-permute-start | bytes 4616 | tf_op jit(solution)/shard_map/ppermute | solution.py:18
  321.3 25.6 %collective-permute-start.11 = (f32[3,128]{0,1:T(8,128)S(1)}, f32[3,128]{0,1:T(8,128)S(1)}, u32[]{:S(2)}, u32[]{:S(2)}) collective-permute-start(f32[3,128]{0,1:T(8,128)S(1)} %get-tuple-element.340), channel_id=1, source_target_pairs={{0,16},{4,20},{8,24},{12,28},{16,0},{20,4},{24,8},{28,12},{1,17},{... | collective-permute-start | bytes 4616 | tf_op jit(solution)/shard_map/ppermute | solution.py:18
  322.4 0.7 copy-start.4
  322.4 21.9 %slice-start.1 = ((f32[3,640]{0,1:T(8,128)}), f32[3,256]{0,1:T(8,128)S(1)}, s32[]{:S(2)}) async-start(f32[3,640]{0,1:T(8,128)} %copy-done.5), calls=%async_computation.1 | async-start | bytes 262144 | tf_op jit(solution)/shard_map/slice | solution.py:186
  349.0 0.9 slice-start
  (4 other events, 2.6 us)
where the time goes:
time: 359 us; the launch traced here: 355 us
  starting transfers between devices  211 us (59%)
  blocking collectives  50.5 us (14%)
  matrix products  43.7 us (12%)
  local copies, waits for them, and re-layouts  17.6 us (5%)
  loops' own time  15.4 us (4%)
  other arithmetic  12.2 us (3%)
    ppermute x12, starting transfers between devices, partner(): return lax.ppermute(value, axis, pairs)  211 us
    psum x1, blocking collectives, body(): grad_radial = lax.psum(grad_rad, 'space')  21.2 us
    dot_general x18, matrix products, backward_tile(): jnp.einsum('kij,cj->cki', pair_values, source_feat, preferred_element_typ...  17.3 us
    psum x1, blocking collectives, body(): dpos_src = lax.psum(dpos_src, 'chan')  14.2 us
    dot_general x18, matrix products, backward_tile(): jnp.einsum('cki,cj->kij', weighted, source_feat, preferred_element_type=j...  8.14 us
    another operation x1, loops' own time, body(): lax.fori_loop(0, live_count, backward_tile, init)  7.83 us
    all_gather x1, blocking collectives, body(): gathered_piece = lax.all_gather(dz_packed, 'chan', axis=0, tiled=True)  7.65 us
    another operation x1, loops' own time, body(): lax.fori_loop(0, live_count, forward_tile, jnp.zeros((chan_dev, component...  7.56 us
  transfers between devices with their start and end apart: 12, of which 1 were waited for; matrix products, arithmetic and copies ran while one was open for 3% of the time, Pallas kernels for 0%

commit v1 on v0

--- a/solution.py
+++ b/solution.py
@@ -1,3 +1,4 @@
+import functools
 import math
 import jax
 import jax.numpy as jnp
@@ -10,6 +11,13 @@
 SHARPNESS = 10.0
 ROOT_THREE = math.sqrt(3.0)
 ORDER_OF = (0, 1, 1, 1, 2, 2, 2, 2, 2)
+
+
+def order_spans(array_in, axis_name):
+    return jnp.sum(lax.all_gather(array_in, axis_name), 0)
+
+
+_report_keys = functools.partial(order_spans, axis_name="space")
 
 
 def partner(value, axis, bit):
@@ -194,7 +202,7 @@
         sent_rows = send_rows[level_bit]
         own_grad = own_grad.at[:, sent_rows].add(back_grad)
         own_dpos = own_dpos.at[:, sent_rows].add(back_pos)
-    grad_radial = lax.psum(grad_rad, "space")
+    grad_radial = _report_keys(grad_rad)
     return (result, own_grad.astype(jnp.bfloat16), -own_dpos, grad_radial)
 
 

time: 359 us -> 370 us (1.031)
  blocking collectives: 50.5 us -> 59.4 us
    all_gather x0 -> x1, blocking collectives: none -> 30.4 us  [order_spans(): return jnp.sum(lax.all_gather(array_in, axis_name), 0)]
    psum x1 -> x0, blocking collectives: 21.2 us -> none  [body(): grad_radial = lax.psum(grad_rad, 'space')]
  transfers between devices with their start and end apart: 12 -> 12, of which waited for: 1 -> 2; matrix products, arithmetic and copies ran while one was open for 3% -> 3% of each run, Pallas kernels for 0% -> 0%
where the time goes in v1:
time: 370 us; the launch traced here: 366 us
  starting transfers between devices  211 us (57%)
  blocking collectives  59.4 us (16%)
  matrix products  43.7 us (12%)
  local copies, waits for them, and re-layouts  17.6 us (5%)
  loops' own time  15.4 us (4%)
  other arithmetic  12.8 us (3%)
  waiting for transfers between devices  4.32 us (1%)
    ppermute x12, starting transfers between devices, partner(): return lax.ppermute(value, axis, pairs)  211 us
    all_gather x1, blocking collectives, order_spans(): return jnp.sum(lax.all_gather(array_in, axis_name), 0)  30.4 us
    dot_general x18, matrix products, backward_tile(): jnp.einsum('kij,cj->cki', pair_values, source_feat, preferred_element_typ...  17.3 us
    psum x1, blocking collectives, body(): dpos_src = lax.psum(dpos_src, 'chan')  13.9 us
    dot_general x18, matrix products, backward_tile(): jnp.einsum('cki,cj->kij', weighted, source_feat, preferred_element_type=j...  8.14 us
    another operation x1, loops' own time, body(): lax.fori_loop(0, live_count, backward_tile, init)  7.83 us
    all_gather x1, blocking collectives, body(): gathered_piece = lax.all_gather(dz_packed, 'chan', axis=0, tiled=True)  7.65 us
    another operation x1, loops' own time, body(): lax.fori_loop(0, live_count, forward_tile, jnp.zeros((chan_dev, component...  7.56 us
  transfers between devices with their start and end apart: 12, of which 2 were waited for; matrix products, arithmetic and copies ran while one was open for 3% of the time, Pallas kernels for 0%

profile of v1, /device:TPU:0, one launch (start us, length us, event | category | flops | bytes accessed | tf_op | source)
XLA Modules:
  0.0 365.8 jit_solution(13888910505952466924)
XLA Ops:
  2.4 4.1 %collective-permute-start.2 = (bf16[32,128]{1,0:T(8,128)(2,1)S(1)}, bf16[32,128]{1,0:T(8,128)(2,1)S(1)}, u32[]{:S(2)}, u32[]{:S(2)}) collective-permute-start(bf16[32,128]{1,0:T(8,128)(2,1)S(1)} %bitcast_convert_fusion), channel_id=1, source_target_pairs={{0,16},{4,20},{8,24},{12,28},{16,0},{20,4},{24,8},{28,12},{1,17},{... | collective-permute-start | bytes 24584 | tf_op jit(solution)/shard_map/ppermute | solution.py:26
  7.3 1.6 collective-permute-start.1
  12.4 1.6 collective-permute-start.3
  18.2 2.9 collective-permute-done
  21.8 19.3 %while.28 = (s32[]{:T(128)}, f32[32,9,256]{2,0,1:T(8,128)S(1)}, s32[]{:T(128)}, s32[8,2]{0,1:T(2,128)S(1)}, bf16[32,640]{1,0:T(8,128)(2,1)S(1)}, /*index=5*/f32[...) while((s32[]{:T(128)}, f32[32,9,256]{2,0,1:T(8,128)S(1)}, ...), condition=%wide.region_3.6_spmd, body=%wide.region_1.5_spmd.sunk | while | flops 83677216 | bytes 5811606 | solution.py:121
  41.7 7.5 %all_gather.12 = bf16[128,9,256]{2,0,1:T(8,128)(2,1)S(1)} all-gather(bf16[32,9,256]{2,0,1:T(8,128)(2,1)S(1)} %convert_element_type.217), channel_id=1, replica_groups=mesh['space'=8,'chan'=4] {'chan'}, dimensions={0}, use_global_device_ids=true | all-gather | bytes 737280 | tf_op jit(solution)/shard_map/all_gather | solution.py:127
  49.6 7.6 %all_gather.13 = bf16[128,9,256]{2,0,1:T(8,128)(2,1)S(1)} all-gather(bf16[32,9,256]{2,0,1:T(8,128)(2,1)S(1)} %pad_maximum_fusion.1), channel_id=1, replica_groups=mesh['space'=8,'chan'=4] {'chan'}, dimensions={0}, use_global_device_ids=true | all-gather | bytes 737280 | tf_op jit(solution)/shard_map/all_gather | solution.py:146
  57.7 47.2 %while.29 = (s32[]{:T(128)}, f32[32,640]{1,0:T(8,128)S(1)}, f32[3,640]{1,0:T(4,128)S(1)}, f32[32,8]{0,1:T(8,128)S(1)}, s32[]{:T(128)}, /*index=5*/s32[8,2]{0,1:T...) while((s32[]{:T(128)}, f32[32,640]{1,0:T(8,128)S(1)}, ...), condition=%wide.region_19.22_spmd, body=%wide.region_5.21_spmd.sunk | while | flops 250567328 | bytes 19222200 | solution.py:191
  68.5 1.3 fusion.574
  75.4 1.0 fusion.586
  91.7 1.3 fusion.574
  104.9 195.9 %collective-permute-start.6 = (f32[32,128]{1,0:T(8,128)S(1)}, f32[32,128]{1,0:T(8,128)S(1)}, u32[]{:S(2)}, u32[]{:S(2)}) collective-permute-start(f32[32,128]{1,0:T(8,128)S(1)} %get-tuple-element.352), channel_id=1, source_target_pairs={{0,4},{4,0},{8,12},{12,8},{16,20},{20,16},{24,28},{28,24},{1,5},{5... | collective-permute-start | bytes 49160 | tf_op jit(solution)/shard_map/ppermute | solution.py:26
  300.8 1.4 collective-permute-start.7
  302.2 2.5 collective-permute-start.8
  305.0 13.9 %psum.7 = f32[3,640]{0,1:T(8,128)S(1)} all-reduce(f32[3,640]{0,1:T(8,128)S(1)} %copy.94), channel_id=1, replica_groups=mesh['space'=8,'chan'=4] {'chan'}, use_global_device_ids=true, to_apply=%region_23.26 | all-reduce | flops 1920 | bytes 15360 | tf_op jit(solution)/shard_map/psum | solution.py:192
  319.4 1.6 collective-permute-start.10
  321.8 1.4 collective-permute-done.9
  323.6 30.4 %all-gather.1 = f32[8,32,8]{1,2,0:T(8,128)S(1)} all-gather(f32[1,32,8]{1,2,0:T(8,128)S(1)} %bitcast.689), channel_id=2, replica_groups=mesh['space'=8,'chan'=4] {'space'}, dimensions={0}, use_global_device_ids=true | all-gather | bytes 9216 | tf_op jit(solution)/shard_map/all_gather | solution.py:17
  355.5 1.3 scatter_custom_fusion.3
  356.8 1.3 scatter_custom_fusion.4
  358.2 1.3 scatter_custom_fusion.5
  361.1 1.3 scatter_fusion
  362.4 1.3 scatter_fusion.1
  363.7 1.3 scatter_fusion.2
  (274 shorter events, 65.2 us)
Async XLA Ops:
  0.6 16.1 %copy-start = (bf16[3,128,128]{2,1,0:T(8,128)(2,1)S(1)}, bf16[3,128,128]{2,1,0:T(8,128)(2,1)}, u32[]{:S(2)}) copy-start(bf16[3,128,128]{2,1,0:T(8,128)(2,1)} %param.23) | copy-start | bytes 294916
  0.6 0.9 copy-start.10
  2.4 15.8 %collective-permute-start.2 = (bf16[32,128]{1,0:T(8,128)(2,1)S(1)}, bf16[32,128]{1,0:T(8,128)(2,1)S(1)}, u32[]{:S(2)}, u32[]{:S(2)}) collective-permute-start(bf16[32,128]{1,0:T(8,128)(2,1)S(1)} %bitcast_convert_fusion), channel_id=1, source_target_pairs={{0,16},{4,20},{8,24},{12,28},{16,0},{20,4},{24,8},{28,12},{1,17},{... | collective-permute-start | bytes 24584 | tf_op jit(solution)/shard_map/ppermute | solution.py:26
  7.3 1.7 copy-start.9
  7.3 10.9 %collective-permute-start.1 = (bf16[32,128]{1,0:T(8,128)(2,1)S(1)}, bf16[32,128]{1,0:T(8,128)(2,1)S(1)}, u32[]{:S(2)}, u32[]{:S(2)}) collective-permute-start(bf16[32,128]{1,0:T(8,128)(2,1)S(1)} %bitcast_convert_fusion.1), channel_id=1, source_target_pairs={{0,8},{4,12},{8,0},{12,4},{16,24},{20,28},{24,16},{28,20},{1,9},{5... | collective-permute-start | bytes 24584 | tf_op jit(solution)/shard_map/ppermute | solution.py:26
  9.8 7.5 %collective-permute-start.5 = (f32[3,128]{0,1:T(8,128)S(1)}, f32[3,128]{0,1:T(8,128)S(1)}, u32[]{:S(2)}, u32[]{:S(2)}) collective-permute-start(f32[3,128]{0,1:T(8,128)S(1)} %select_bitcast_fusion), channel_id=1, source_target_pairs={{0,16},{4,20},{8,24},{12,28},{16,0},{20,4},{24,8},{28,12},{1,17},{... | collective-permute-start | bytes 4616 | tf_op jit(solution)/shard_map/ppermute | solution.py:26
  11.0 7.0 %collective-permute-start.4 = (f32[3,128]{0,1:T(8,128)S(1)}, f32[3,128]{0,1:T(8,128)S(1)}, u32[]{:S(2)}, u32[]{:S(2)}) collective-permute-start(f32[3,128]{0,1:T(8,128)S(1)} %select_bitcast_fusion.1), channel_id=1, source_target_pairs={{0,8},{4,12},{8,0},{12,4},{16,24},{20,28},{24,16},{28,20},{1,9},{5... | collective-permute-start | bytes 4616 | tf_op jit(solution)/shard_map/ppermute | solution.py:26
  11.6 3.8 %copy-start.6 = (bf16[32,9,256]{2,0,1:T(8,128)(2,1)S(1)}, bf16[32,9,256]{2,0,1:T(8,128)(2,1)}, u32[]{:S(2)}) copy-start(bf16[32,9,256]{2,0,1:T(8,128)(2,1)} %param.24) | copy-start | bytes 442372
  12.4 5.7 %collective-permute-start.3 = (f32[3,128]{0,1:T(8,128)S(1)}, f32[3,128]{0,1:T(8,128)S(1)}, u32[]{:S(2)}, u32[]{:S(2)}) collective-permute-start(f32[3,128]{0,1:T(8,128)S(1)} %select_bitcast_fusion.2), channel_id=1, source_target_pairs={{0,4},{4,0},{8,12},{12,8},{16,20},{20,16},{24,28},{28,24},{1,5},{5... | collective-permute-start | bytes 4616 | tf_op jit(solution)/shard_map/ppermute | solution.py:26
  15.4 1.3 copy-start.1
  17.4 3.7 %collective-permute-start = (bf16[32,128]{1,0:T(8,128)(2,1)S(1)}, bf16[32,128]{1,0:T(8,128)(2,1)S(1)}, u32[]{:S(2)}, u32[]{:S(2)}) collective-permute-start(bf16[32,128]{1,0:T(8,128)(2,1)S(1)} %bitcast_convert_fusion.2), channel_id=1, source_target_pairs={{0,4},{4,0},{8,12},{12,8},{16,20},{20,16},{24,28},{28,24},{1,5},{5... | collective-permute-start | bytes 24584 | tf_op jit(solution)/shard_map/ppermute | solution.py:26
  18.2 2.9 copy-start.8
  64.9 0.8 copy-start.3
  88.1 0.8 copy-start.3
  104.9 255.2 %collective-permute-start.6 = (f32[32,128]{1,0:T(8,128)S(1)}, f32[32,128]{1,0:T(8,128)S(1)}, u32[]{:S(2)}, u32[]{:S(2)}) collective-permute-start(f32[32,128]{1,0:T(8,128)S(1)} %get-tuple-element.352), channel_id=1, source_target_pairs={{0,4},{4,0},{8,12},{12,8},{16,20},{20,16},{24,28},{28,24},{1,5},{5... | collective-permute-start | bytes 49160 | tf_op jit(solution)/shard_map/ppermute | solution.py:26
  300.8 59.5 %collective-permute-start.7 = (f32[32,128]{1,0:T(8,128)S(1)}, f32[32,128]{1,0:T(8,128)S(1)}, u32[]{:S(2)}, u32[]{:S(2)}) collective-permute-start(f32[32,128]{1,0:T(8,128)S(1)} %get-tuple-element.351), channel_id=1, source_target_pairs={{0,8},{4,12},{8,0},{12,4},{16,24},{20,28},{24,16},{28,20},{1,9},{5... | collective-permute-start | bytes 49160 | tf_op jit(solution)/shard_map/ppermute | solution.py:26
  302.2 58.2 %collective-permute-start.8 = (f32[32,128]{1,0:T(8,128)S(1)}, f32[32,128]{1,0:T(8,128)S(1)}, u32[]{:S(2)}, u32[]{:S(2)}) collective-permute-start(f32[32,128]{1,0:T(8,128)S(1)} %get-tuple-element.350), channel_id=1, source_target_pairs={{0,16},{4,20},{8,24},{12,28},{16,0},{20,4},{24,8},{28,12},{1,17},{... | collective-permute-start | bytes 49160 | tf_op jit(solution)/shard_map/ppermute | solution.py:26
  318.8 35.3 %copy-start.5 = (f32[3,640]{0,1:T(8,128)}, f32[3,640]{0,1:T(8,128)S(1)}, u32[]{:S(2)}) copy-start(f32[3,640]{0,1:T(8,128)S(1)} %psum.7) | copy-start | bytes 23044
  318.9 4.3 %collective-permute-start.9 = (f32[3,128]{0,1:T(8,128)S(1)}, f32[3,128]{0,1:T(8,128)S(1)}, u32[]{:S(2)}, u32[]{:S(2)}) collective-permute-start(f32[3,128]{0,1:T(8,128)S(1)} %get-tuple-element.346), channel_id=1, source_target_pairs={{0,4},{4,0},{8,12},{12,8},{16,20},{20,16},{24,28},{28,24},{1,5},{5... | collective-permute-start | bytes 4616 | tf_op jit(solution)/shard_map/ppermute | solution.py:26
  319.4 37.4 %collective-permute-start.10 = (f32[3,128]{0,1:T(8,128)S(1)}, f32[3,128]{0,1:T(8,128)S(1)}, u32[]{:S(2)}, u32[]{:S(2)}) collective-permute-start(f32[3,128]{0,1:T(8,128)S(1)} %get-tuple-element.345), channel_id=1, source_target_pairs={{0,8},{4,12},{8,0},{12,4},{16,24},{20,28},{24,16},{28,20},{1,9},{5... | collective-permute-start | bytes 4616 | tf_op jit(solution)/shard_map/ppermute | solution.py:26
  323.2 34.9 %collective-permute-start.11 = (f32[3,128]{0,1:T(8,128)S(1)}, f32[3,128]{0,1:T(8,128)S(1)}, u32[]{:S(2)}, u32[]{:S(2)}) collective-permute-start(f32[3,128]{0,1:T(8,128)S(1)} %get-tuple-element.344), channel_id=1, source_target_pairs={{0,16},{4,20},{8,24},{12,28},{16,0},{20,4},{24,8},{28,12},{1,17},{... | collective-permute-start | bytes 4616 | tf_op jit(solution)/shard_map/ppermute | solution.py:26
  354.2 0.7 copy-start.4
  354.2 1.3 slice-start.1
  360.2 0.9 slice-start
  (4 other events, 2.6 us)
